TPU v7x, 512 devices: a whole 4x8x8 slice. The times are simulated.
512 devices in a mesh: dp: 64 (over z, x, core), mp: 8 (over y).
Axes of the slice: x: 4, y: 8, z: 8, core: 2. Of those that a mesh axis runs over, the one named last changes fastest.
Arguments:
- micro_grads: bfloat16 [64, 2, 768, 768], P('dp', None, None, 'mp'), may hold values from -16 to 16
- master: float32 [768, 768], P('dp', 'mp'), may hold values from -0.21875 to 0.21875
- moment: float32 [768, 768], P('dp', 'mp'), may hold values from -1.5 to 1.5
- second: float32 [768, 768], P('dp', 'mp'), may hold values from 0.001 to 0.1
- left_basis: float32 [768, 768], P(None, 'dp'), may hold values from -0.21875 to 0.21875
- right_basis: float32 [768, 768], P(None, 'mp'), may hold values from -0.21875 to 0.21875
- left_stat: float32 [768, 768], P('mp'), may hold values from -2 to 5, as said below
- right_stat: float32 [768, 768], P('mp'), may hold values from -2 to 5, as said below
Outputs:
- weights_block: bfloat16 [768, 768], P(None, 'mp')
- new_master: float32 [768, 768], P('dp', 'mp')
- new_moment: float32 [768, 768], P('dp', 'mp')
- new_second: float32 [768, 768], P('dp', 'mp')
- new_left_stat: float32 [768, 768], P('mp')
- new_right_stat: float32 [768, 768], P('mp')
- new_left_basis: float32 [768, 768], P('mp')
- new_right_basis: float32 [768, 768], P('mp')
Inputs may be any that keep to these rules, and one draw needn't show every extreme that they name: `left_stat`: symmetric. `right_stat`: symmetric.
All inputs are finite; a program needn't handle non-finite values.
Results may differ from a plain program's by a relative error of at most 0.004.
The roundings to bfloat16 on the way count: a program that leaves them out, or rounds other values in their place, can miss the bound.
Values may be sent and summed in bfloat16 or wider, within the bound.
No kernel may reach another device: no remote copies, remote signals or barrier semaphores. Data moves between devices by JAX's collectives and lax.ppermute only.
A program may use at most 64 MiB of HBM per device.

v0:
```python
import jax
import jax.numpy as jnp
from jax import lax
from jax.sharding import PartitionSpec as P

beta_one = 0.9
beta_two = 0.95
beta_stat = 0.95
learn_rate = 0.02
adam_eps = 1e-08
norm_eps = 1e-06
quint_a = 1.875
quint_b = -1.25
quint_c = 0.375
highest = lax.Precision.HIGHEST


def for_sending(x):

    def short(part):
        return part.astype(jnp.bfloat16) if part.dtype == jnp.float32 else part

    return jax.tree.map(short, x)


def all_rows(pair):
    return jax.tree.map(
        lambda part, own: part.astype(own.dtype),
        lax.all_gather(for_sending(pair), "mp", axis=0, tiled=True),
        pair,
    )


def row_gram(row_part, whole_part):
    return lax.dot_general(
        row_part, whole_part, (((1,), (1,)), ((), ())), preferred_element_type=jnp.float32
    )


def per_device(micro_grads, master, moment, second, left_basis, right_basis, left_stat, right_stat):
    dp_count = lax.axis_size("dp")
    micro_count = micro_grads.shape[1]
    local_sum = jnp.sum(micro_grads[0], axis=0, dtype=jnp.float32)
    grad_piece = lax.psum_scatter(local_sum, "dp", scatter_dimension=0, tiled=True) / (
        micro_count * dp_count
    )
    new_moment = beta_one * moment + (1.0 - beta_one) * grad_piece
    grad_cols, moment_cols, left_full = (
        lax.all_gather(grad_piece, "dp", axis=0, tiled=True),
        lax.all_gather(new_moment, "dp", axis=0, tiled=True),
        lax.all_gather(left_basis, "dp", axis=1, tiled=True),
    )
    grad_full, moment_full, right_full = (
        lax.all_gather(grad_cols, "mp", axis=1, tiled=True),
        lax.all_gather(moment_cols, "mp", axis=1, tiled=True),
        lax.all_gather(right_basis, "mp", axis=1, tiled=True),
    )

    def rotate(matrix):
        left_part = lax.dot_general(left_basis, matrix, (((0,), (0,)), ((), ())), precision=highest)
        return jnp.dot(left_part, right_basis, precision=highest)

    rot_grad = rotate(grad_full)
    rot_moment = rotate(moment_full)
    new_second = beta_two * second + (1.0 - beta_two) * rot_grad * rot_grad
    rot_step = rot_moment / (jnp.sqrt(new_second) + adam_eps)
    basis_rows = right_basis
    back_half = lax.psum_scatter(
        lax.dot_general(basis_rows, rot_step, (((1,), (1,)), ((), ())), precision=highest),
        "mp",
        scatter_dimension=0,
        tiled=True,
    )
    basis_rows = left_basis
    step_piece = lax.psum_scatter(
        lax.dot_general(basis_rows, back_half, (((1,), (1,)), ((), ())), precision=highest),
        "dp",
        scatter_dimension=0,
        tiled=True,
    )
    new_master = master - learn_rate * step_piece
    weights_block = lax.all_gather(new_master.astype(jnp.bfloat16), "dp", axis=0, tiled=True)
    band_width = right_basis.shape[1]
    band_start = lax.axis_index("mp") * band_width
    grad_band = lax.dynamic_slice_in_dim(grad_full, band_start, band_width, 0)
    grad_strip = lax.dynamic_slice_in_dim(grad_full, band_start, band_width, 1)
    left_outer = lax.dot_general(grad_band, grad_full, (((1,), (1,)), ((), ())), precision=highest)
    right_outer = lax.dot_general(
        grad_strip, grad_full, (((0,), (0,)), ((), ())), precision=highest
    )
    new_left_stat = beta_stat * left_stat + (1.0 - beta_stat) * left_outer
    new_right_stat = beta_stat * right_stat + (1.0 - beta_stat) * right_outer
    order_count = left_stat.shape[1]
    power_left = jnp.dot(
        new_left_stat.astype(jnp.bfloat16),
        left_full.astype(jnp.bfloat16),
        preferred_element_type=jnp.float32,
    )
    power_right = jnp.dot(
        new_right_stat.astype(jnp.bfloat16),
        right_full.astype(jnp.bfloat16),
        preferred_element_type=jnp.float32,
    )
    total_left, total_right = lax.psum(
        (jnp.sum(power_left * power_left), jnp.sum(power_right * power_right)), "mp"
    )
    start_left = lax.optimization_barrier(
        (power_left * lax.rsqrt(total_left * (4.0 / order_count) + norm_eps)).astype(jnp.bfloat16)
    )
    start_right = lax.optimization_barrier(
        (power_right * lax.rsqrt(total_right * (4.0 / order_count) + norm_eps)).astype(jnp.bfloat16)
    )
    start_rows = (start_left, start_right)
    start_whole = all_rows(start_rows)
    gram_rows = tuple(
        (
            lax.optimization_barrier(row_gram(row_part, whole_part).astype(jnp.bfloat16))
            for row_part, whole_part in zip(start_rows, start_whole)
        )
    )
    gram_whole = all_rows(gram_rows)
    middle_rows = []
    for row_part, gram_part, gram_all, whole_part in zip(
        start_rows, gram_rows, gram_whole, start_whole
    ):
        square = jnp.dot(gram_part, gram_all, preferred_element_type=jnp.float32)
        poly_rows = (quint_b * gram_part.astype(jnp.float32) + quint_c * square).astype(
            jnp.bfloat16
        )
        middle = quint_a * row_part.astype(jnp.float32) + jnp.dot(
            poly_rows, whole_part, preferred_element_type=jnp.float32
        )
        middle_rows.append(lax.optimization_barrier(middle.astype(jnp.bfloat16)))
    middle_whole = all_rows(tuple(middle_rows))
    new_bases = []
    for row_part, whole_part in zip(middle_rows, middle_whole):
        gram_two = row_gram(row_part, whole_part).astype(jnp.bfloat16)
        new_bases.append(
            1.5 * row_part.astype(jnp.float32)
            - 0.5 * jnp.dot(gram_two, whole_part, preferred_element_type=jnp.float32)
        )
    return (
        weights_block,
        new_master,
        new_moment,
        new_second,
        new_left_stat,
        new_right_stat,
        new_bases[0],
        new_bases[1],
    )


def solution(mesh):
    in_specs = (
        P("dp", None, None, "mp"),
        P("dp", "mp"),
        P("dp", "mp"),
        P("dp", "mp"),
        P(None, "dp"),
        P(None, "mp"),
        P("mp", None),
        P("mp", None),
    )
    out_specs = (
        P(None, "mp"),
        P("dp", "mp"),
        P("dp", "mp"),
        P("dp", "mp"),
        P("mp", None),
        P("mp", None),
        P("mp", None),
        P("mp", None),
    )
    return jax.shard_map(
        per_device, mesh=mesh, in_specs=in_specs, out_specs=out_specs, check_vma=False
    )
```

profile of v0, /device:TPU:2, one launch (start us, length us, event | category | flops | bytes accessed | tf_op | source)
XLA Modules:
  0.0 924.6 jit_solution(14783238774417573509)
XLA Ops:
  7.2 1.0 convert_reduce_fusion
  8.3 0.9 copy.22
  9.3 0.6 bitcast_convert_fusion
  10.0 1.3 dynamic-slice
  12.0 195.7 %all-reduce.6.cloned.1.call-done = f32[768,96]{1,0:T(8,128)} async-done(((f32[768,96]{1,0:T(8,128)}), f32[768,96]{1,0:T(8,128)}) %all-reduce.6.cloned.1.call-update) | async-done | bytes 294928
  207.6 0.7 multiply_bitcast_fusion
  208.4 48.3 %all-gather.1 = f32[64,12,96]{2,1,0:T(8,128)S(1)} all-gather(f32[1,12,96]{2,1,0:T(8,128)S(1)} %get-tuple-element.36), channel_id=1, replica_groups=mesh['dp'=64,'mp'=8] {'dp'}, dimensions={0}, use_global_device_ids=true | all-gather | bytes 299520 | tf_op jit(solution)/shard_map/all_gather | solution.py:49
  256.7 0.9 copy.24
  257.6 0.7 convert.1
  258.4 48.9 %all-gather = f32[64,12,96]{2,1,0:T(8,128)S(1)} all-gather(f32[1,12,96]{2,1,0:T(8,128)S(1)} %bitcast.49), channel_id=1, replica_groups=mesh['dp'=64,'mp'=8] {'dp'}, dimensions={0}, use_global_device_ids=true | all-gather | bytes 299520 | tf_op jit(solution)/shard_map/all_gather | solution.py:50
  307.3 0.9 copy.23
  308.3 3.2 reshape.25
  311.5 26.6 %all-gather.17.cloned.1.call-done = f32[768,768]{0,1:T(8,128)} async-done(((f32[768,96]{0,1:T(8,128)}), f32[768,768]{0,1:T(8,128)}) %all-gather.17.cloned.1.call-update) | async-done | bytes 2359312 | tf_op jit(solution)/shard_map/all_gather | solution.py:54
  338.2 3.7 fusion.3
  341.9 3.2 multiply_reduce_fusion.1
  345.1 2.4 fusion.2
  347.5 33.6 %all-gather.25.cloned.1.call-done = bf16[768,768]{0,1:T(8,128)(2,1)} async-done(((bf16[768,96]{0,1:T(8,128)(2,1)}), bf16[768,768]{0,1:T(8,128)(2,1)}) %all-gather.25.cloned.1.call-update) | async-done | bytes 1179664 | tf_op jit(solution)/shard_map/all_gather | solution.py:56
  381.1 2.4 multiply_reduce_fusion
  383.5 16.6 %all-reduce.2 = (f32[]{:T(128)}, f32[]{:T(128)}) all-reduce(f32[]{:T(128)} %get-tuple-element.38, f32[]{:T(128)} %get-tuple-element.40), channel_id=1, replica_groups=mesh['dp'=64,'mp'=8] {'mp'}, use_global_device_ids=true, to_apply=%region_5.0 | all-reduce | flops 2 | bytes 16 | tf_op jit(solution)/shard_map/psum | solution.py:104
  400.8 0.7 multiply_convert_fusion.1
  402.2 0.7 multiply_convert_fusion
  403.0 0.2 reduce-scatter.5.cloned.1.call-start
  403.2 2.8 fusion.35
  406.0 0.3 fusion.26
  406.4 20.7 %all-gather.15.cloned.1.call-done = f32[768,768]{0,1:T(8,128)} async-done(((f32[768,96]{0,1:T(8,128)}), f32[768,768]{0,1:T(8,128)}) %all-gather.15.cloned.1.call-update) | async-done | bytes 2359312 | tf_op jit(solution)/shard_map/all_gather | solution.py:55
  427.1 3.7 fusion.34
  430.8 0.3 convolution_divide_fusion
  431.1 0.3 convolution_bitcast_fusion.1
  431.5 1.0 copy.29
  432.5 37.3 %all-gather.19.cloned.1.call-done = bf16[768,768]{1,0:T(8,128)(2,1)} async-done(((bf16[96,768]{1,0:T(8,128)(2,1)}), bf16[768,768]{1,0:T(8,128)(2,1)}) %all-gather.19.cloned.1.call-update) | async-done | bytes 1179664 | tf_op jit(solution)/shard_map/all_gather | solution.py:29
  469.8 2.4 convolution_convert_fusion.3
  472.4 40.6 %all-gather.27.cloned.1.call-done = bf16[768,768]{1,0:T(8,128)(2,1)} async-done(((bf16[96,768]{1,0:T(8,128)(2,1)}), bf16[768,768]{1,0:T(8,128)(2,1)}) %all-gather.27.cloned.1.call-update) | async-done | bytes 1179664 | tf_op jit(solution)/shard_map/all_gather | solution.py:29
  512.9 2.4 convolution_convert_fusion.1
  515.4 38.7 %reduce-scatter.5.cloned.1.call-done = f32[96,12]{1,0:T(8,128)} async-done(((f32[768,12]{1,0:T(8,128)}), f32[96,12]{1,0:T(8,128)}) %reduce-scatter.5.cloned.1.call-update) | async-done | bytes 4624
  554.2 1.9 convolution_bitcast_fusion
  556.1 41.1 %all-gather.21.cloned.1.call-done = bf16[768,768]{1,0:T(8,128)(2,1)} async-done(((bf16[96,768]{1,0:T(8,128)(2,1)}), bf16[768,768]{1,0:T(8,128)(2,1)}) %all-gather.21.cloned.1.call-update) | async-done | bytes 1179664 | tf_op jit(solution)/shard_map/all_gather | solution.py:29
  597.3 2.5 fusion.9
  599.9 39.5 %all-gather.29.cloned.1.call-done = bf16[768,768]{1,0:T(8,128)(2,1)} async-done(((bf16[96,768]{1,0:T(8,128)(2,1)}), bf16[768,768]{1,0:T(8,128)(2,1)}) %all-gather.29.cloned.1.call-update) | async-done | bytes 1179664 | tf_op jit(solution)/shard_map/all_gather | solution.py:29
  639.4 2.5 fusion.11
  642.0 0.1 copy.25
  642.1 187.5 %all-reduce.8.cloned.1.call-done = f32[768,96]{0,1:T(8,128)} async-done(((f32[768,96]{0,1:T(8,128)}), f32[768,96]{0,1:T(8,128)}) %all-reduce.8.cloned.1.call-update) | async-done | bytes 294928
  829.7 1.0 convert_bitcast_fusion
  830.7 41.5 %all-gather.2 = bf16[64,12,96]{2,1,0:T(8,128)(2,1)S(1)} all-gather(bf16[1,12,96]{2,1,0:T(8,128)(2,1)S(1)} %copy.26), channel_id=1, replica_groups=mesh['dp'=64,'mp'=8] {'dp'}, dimensions={0}, use_global_device_ids=true | all-gather | bytes 149760 | tf_op jit(solution)/shard_map/all_gather | solution.py:82
  872.3 0.8 copy.27
  873.1 0.7 copy.28
  873.7 3.1 fusion.6
  876.9 38.0 %all-gather.31.cloned.1.call-done = bf16[768,768]{1,0:T(8,128)(2,1)} async-done(((bf16[96,768]{1,0:T(8,128)(2,1)}), bf16[768,768]{1,0:T(8,128)(2,1)}) %all-gather.31.cloned.1.call-update) | async-done | bytes 1179664 | tf_op jit(solution)/shard_map/all_gather | solution.py:29
  914.9 3.1 fusion.4
  (75 shorter events, 1.2 us)
Async XLA Ops:
  7.2 2.1 copy-start.13
  7.2 200.5 %copy-start.21 = (f32[12,96]{1,0:T(8,128)S(1)}, f32[12,96]{1,0:T(8,128)}, u32[]{:S(2)}) copy-start(f32[12,96]{1,0:T(8,128)} %param.10) | copy-start | bytes 13828
  7.2 200.4 %all-reduce.6.cloned.1.call-start = ((), (), s32[]{:S(2)}) async-start(), calls=%async_computation.12 | async-start | bytes 786432
  9.2 299.1 %all-gather.33.cloned.1.call-start = ((), (), s32[]{:S(2)}) async-start(), calls=%async_computation.10 | async-start | bytes 1597440 | tf_op jit(solution)/shard_map/all_gather | solution.py:51
  10.0 328.2 %all-gather.17.cloned.1.call-start = ((), (), s32[]{:S(2)}) async-start(), calls=%async_computation.2 | async-start | bytes 2654208 | tf_op jit(solution)/shard_map/all_gather | solution.py:54
  208.3 50.0 %copy-start.17 = (f32[12,96]{1,0:T(8,128)}, f32[12,96]{1,0:T(8,128)S(1)}, u32[]{:S(2)}) copy-start(f32[12,96]{1,0:T(8,128)S(1)} %get-tuple-element.37) | copy-start | bytes 13828
  208.3 49.3 %copy-start.1 = (f32[768,96]{0,1:T(8,128)S(1)}, f32[768,96]{0,1:T(8,128)}, u32[]{:S(2)}) copy-start(f32[768,96]{0,1:T(8,128)} %param.13) | copy-start | bytes 884740
  257.6 123.5 %all-gather.25.cloned.1.call-start = ((), (), s32[]{:S(2)}) async-start(), calls=%async_computation.6 | async-start | bytes 1327104 | tf_op jit(solution)/shard_map/all_gather | solution.py:56
  258.3 168.8 %all-gather.15.cloned.1.call-start = ((), (), s32[]{:S(2)}) async-start(), calls=%async_computation.1 | async-start | bytes 2654208 | tf_op jit(solution)/shard_map/all_gather | solution.py:55
  308.2 161.6 %all-gather.19.cloned.1.call-start = ((), (), s32[]{:S(2)}) async-start(), calls=%async_computation.3 | async-start | bytes 1327104 | tf_op jit(solution)/shard_map/all_gather | solution.py:29
  308.3 29.9 %copy-start.15 = (f32[96,768]{1,0:T(8,128)S(1)}, f32[96,768]{1,0:T(8,128)}, u32[]{:S(2)}) copy-start(f32[96,768]{1,0:T(8,128)} %param.14) | copy-start | bytes 884740
  338.2 6.9 copy-start
  341.8 5.6 copy-start.10
  341.9 3.2 copy-start.16
  347.5 54.0 %copy-start.11 = (f32[96,768]{1,0:T(8,128)}, f32[96,768]{1,0:T(8,128)S(1)}, u32[]{:S(2)}) copy-start(f32[96,768]{1,0:T(8,128)S(1)} %fusion.2) | copy-start | bytes 884740
  381.1 19.7 %copy-start.12 = (f32[96,768]{1,0:T(8,128)S(1)}, f32[96,768]{1,0:T(8,128)}, u32[]{:S(2)}) copy-start(f32[96,768]{1,0:T(8,128)} %get-tuple-element.39) | copy-start | bytes 884740
  401.5 111.4 %all-gather.27.cloned.1.call-start = ((), (), s32[]{:S(2)}) async-start(), calls=%async_computation.7 | async-start | bytes 1327104 | tf_op jit(solution)/shard_map/all_gather | solution.py:29
  402.9 3.1 copy-start.19
  403.0 24.2 %copy-start.14 = (f32[768,12]{0,1:T(8,128)S(1)}, f32[768,12]{0,1:T(8,128)}, u32[]{:S(2)}) copy-start(f32[768,12]{0,1:T(8,128)} %param.12) | copy-start | bytes 110596
  403.0 151.2 %reduce-scatter.5.cloned.1.call-start = ((), (), s32[]{:S(2)}) async-start(), calls=%async_computation.11 | async-start | bytes 442368
  406.4 24.5 %copy-start.18 = (f32[12,96]{1,0:T(8,128)}, f32[12,96]{1,0:T(8,128)S(1)}, u32[]{:S(2)}) copy-start(f32[12,96]{1,0:T(8,128)S(1)} %fusion.26) | copy-start | bytes 13828
  430.8 39.0 %copy-start.4 = (bf16[96,768]{1,0:T(8,128)(2,1)S(1)}, bf16[96,768]{1,0:T(8,128)(2,1)}, u32[]{:S(2)}) copy-start(bf16[96,768]{1,0:T(8,128)(2,1)} %multiply_convert_fusion.1) | copy-start | bytes 442372
  431.4 81.5 %copy-start.5 = (bf16[96,768]{1,0:T(8,128)(2,1)S(1)}, bf16[96,768]{1,0:T(8,128)(2,1)}, u32[]{:S(2)}) copy-start(bf16[96,768]{1,0:T(8,128)(2,1)} %multiply_convert_fusion) | copy-start | bytes 442372
  432.4 164.8 %all-gather.21.cloned.1.call-start = ((), (), s32[]{:S(2)}) async-start(), calls=%async_computation.4 | async-start | bytes 1327104 | tf_op jit(solution)/shard_map/all_gather | solution.py:29
  472.3 125.0 %copy-start.2 = (bf16[768,768]{1,0:T(8,128)(2,1)S(1)}, bf16[768,768]{1,0:T(8,128)(2,1)}, u32[]{:S(2)}) copy-start(bf16[768,768]{1,0:T(8,128)(2,1)} %all-gather.19.cloned.1.call-done) | copy-start | bytes 3538948
  472.3 125.0 %copy-start.8 = (bf16[96,768]{1,0:T(8,128)(2,1)S(1)}, bf16[96,768]{1,0:T(8,128)(2,1)}, u32[]{:S(2)}) copy-start(bf16[96,768]{1,0:T(8,128)(2,1)} %convolution_convert_fusion.3) | copy-start | bytes 442372
  472.3 167.1 %all-gather.29.cloned.1.call-start = ((), (), s32[]{:S(2)}) async-start(), calls=%async_computation.8 | async-start | bytes 1327104 | tf_op jit(solution)/shard_map/all_gather | solution.py:29
  515.4 314.3 %all-reduce.8.cloned.1.call-start = ((), (), s32[]{:S(2)}) async-start(), calls=%async_computation.13 | async-start | bytes 589824
  556.1 83.4 %copy-start.3 = (bf16[768,768]{1,0:T(8,128)(2,1)S(1)}, bf16[768,768]{1,0:T(8,128)(2,1)}, u32[]{:S(2)}) copy-start(bf16[768,768]{1,0:T(8,128)(2,1)} %all-gather.27.cloned.1.call-done) | copy-start | bytes 3538948
  556.1 83.4 %copy-start.7 = (bf16[96,768]{1,0:T(8,128)(2,1)S(1)}, bf16[96,768]{1,0:T(8,128)(2,1)}, u32[]{:S(2)}) copy-start(bf16[96,768]{1,0:T(8,128)(2,1)} %convolution_convert_fusion.1) | copy-start | bytes 442372
  556.1 317.7 %all-gather.23.cloned.1.call-start = ((), (), s32[]{:S(2)}) async-start(), calls=%async_computation.5 | async-start | bytes 1327104 | tf_op jit(solution)/shard_map/all_gather | solution.py:29
  599.8 42.2 %copy-start.20 = (f32[12,96]{1,0:T(8,128)S(1)}, f32[12,96]{1,0:T(8,128)}, u32[]{:S(2)}) copy-start(f32[12,96]{1,0:T(8,128)} %param.9) | copy-start | bytes 13828
  599.8 315.1 %all-gather.31.cloned.1.call-start = ((), (), s32[]{:S(2)}) async-start(), calls=%async_computation.9 | async-start | bytes 1327104 | tf_op jit(solution)/shard_map/all_gather | solution.py:29
  642.0 231.8 %copy-start.6 = (bf16[96,768]{1,0:T(8,128)(2,1)S(1)}, bf16[96,768]{1,0:T(8,128)(2,1)}, u32[]{:S(2)}) copy-start(bf16[96,768]{1,0:T(8,128)(2,1)} %fusion.9) | copy-start | bytes 442372
  873.7 41.2 %copy-start.9 = (bf16[96,768]{1,0:T(8,128)(2,1)S(1)}, bf16[96,768]{1,0:T(8,128)(2,1)}, u32[]{:S(2)}) copy-start(bf16[96,768]{1,0:T(8,128)(2,1)} %fusion.11) | copy-start | bytes 442372
Sparse Core Ops, SparseCore 0:
  11.5 196.1 all-reduce.5
  212.1 80.6 all-gather.32
  295.7 42.4 all-gather.16
  340.9 40.1 all-gather.24
  383.8 43.2 all-gather.14
  429.8 39.9 all-gather.18
  472.7 40.2 all-gather.26
  516.0 38.1 reduce-scatter.4
  556.8 40.4 all-gather.20
  599.2 40.2 all-gather.28
  643.5 186.1 all-reduce.7
  832.4 39.9 all-gather.22
  874.7 40.2 all-gather.30
where the time goes:
time: 925 us
  waiting for transfers between devices  700 us (76%)
  blocking collectives  155 us (17%)
  matrix products  37.2 us (4%)
  between operations  16.2 us (2%)
  local copies, waits for them, and re-layouts  10.1 us (1%)
    unnamed x16, waiting for transfers between devices  422 us
    all_gather x6, waiting for transfers between devices, all_rows(): lax.all_gather(for_sending(pair), 'mp', axis=0, tiled=True)  197 us
    all_gather x1, blocking collectives, per_device(): lax.all_gather(new_moment, 'dp', axis=0, tiled=True)  48.9 us
    all_gather x1, blocking collectives, per_device(): lax.all_gather(grad_piece, 'dp', axis=0, tiled=True)  48.3 us
    all_gather x1, blocking collectives, per_device(): lax.all_gather(new_master.astype(jnp.bfloat16), 'dp', axis=0, tiled=True)  41.5 us
    all_gather x1, waiting for transfers between devices, per_device(): lax.all_gather(right_basis, 'mp', axis=1, tiled=True)  33.6 us
    all_gather x1, waiting for transfers between devices, per_device(): lax.all_gather(grad_cols, 'mp', axis=1, tiled=True)  26.6 us
    all_gather x1, waiting for transfers between devices, per_device(): lax.all_gather(moment_cols, 'mp', axis=1, tiled=True)  20.7 us
  transfers between devices with their start and end apart: 13, of which 11 were waited for; matrix products, arithmetic and copies ran while one was open for 5% of the time, Pallas kernels for 0%

commit v1 on v0

--- a/solution.py
+++ b/solution.py
@@ -51,7 +51,9 @@
         lax.all_gather(left_basis, "dp", axis=1, tiled=True),
     )
     grad_full, moment_full, right_full = (
-        lax.all_gather(grad_cols, "mp", axis=1, tiled=True),
+        jnp.concatenate(
+            lax.all_to_all(jnp.stack([grad_cols] * lax.axis_size("mp")), "mp", 0, 0), axis=1
+        ),
         lax.all_gather(moment_cols, "mp", axis=1, tiled=True),
         lax.all_gather(right_basis, "mp", axis=1, tiled=True),
     )

time: 925 us -> 883 us (0.955)
  waiting for transfers between devices: 700 us -> 652 us
    all_gather x1 -> x0, waiting for transfers between devices: 26.6 us -> none  [per_device(): lax.all_gather(grad_cols, 'mp', axis=1, tiled=True)]
    all_gather x1, waiting for transfers between devices: 33.6 us -> 9.87 us  [per_device(): lax.all_gather(right_basis, 'mp', axis=1, tiled=True)]
    unnamed x16 -> x15, waiting for transfers between devices: 422 us -> 421 us
where the time goes in v1:
time: 883 us; the launch traced here: 882 us
  waiting for transfers between devices  652 us (74%)
  blocking collectives  155 us (18%)
  matrix products  33.8 us (4%)
  between operations  16.5 us (2%)
  local copies, waits for them, and re-layouts  12.8 us (1%)
    unnamed x15, waiting for transfers between devices  421 us
    all_gather x6, waiting for transfers between devices, all_rows(): lax.all_gather(for_sending(pair), 'mp', axis=0, tiled=True)  197 us
    all_gather x1, blocking collectives, per_device(): lax.all_gather(new_moment, 'dp', axis=0, tiled=True)  48.9 us
    all_gather x1, blocking collectives, per_device(): lax.all_gather(grad_piece, 'dp', axis=0, tiled=True)  48.1 us
    all_gather x1, blocking collectives, per_device(): lax.all_gather(new_master.astype(jnp.bfloat16), 'dp', axis=0, tiled=True)  41.5 us
    all_gather x1, waiting for transfers between devices, per_device(): lax.all_gather(moment_cols, 'mp', axis=1, tiled=True)  19.2 us
  transfers between devices with their start and end apart: 13, of which 11 were waited for; matrix products, arithmetic and copies ran while one was open for 5% of the time, Pallas kernels for 0%

profile of v1, /device:TPU:2, one launch (start us, length us, event | category | flops | bytes accessed | tf_op | source)
XLA Modules:
  0.0 882.3 jit_solution(2512761754179447597)
XLA Ops:
  7.2 1.1 convert_reduce_fusion
  8.3 0.9 copy.23
  9.3 0.6 bitcast_convert_fusion
  10.1 0.7 convert.1
  10.8 1.3 dynamic-slice
  12.7 194.9 %all-reduce.6.cloned.1.call-done = f32[768,96]{1,0:T(8,128)} async-done(((f32[768,96]{1,0:T(8,128)}), f32[768,96]{1,0:T(8,128)}) %all-reduce.6.cloned.1.call-update) | async-done | bytes 294928
  207.6 0.7 multiply_bitcast_fusion
  208.4 48.1 %all-gather.1 = f32[64,12,96]{2,1,0:T(8,128)S(1)} all-gather(f32[1,12,96]{2,1,0:T(8,128)S(1)} %get-tuple-element.36), channel_id=1, replica_groups=mesh['dp'=64,'mp'=8] {'dp'}, dimensions={0}, use_global_device_ids=true | all-gather | bytes 299520 | tf_op jit(solution)/shard_map/all_gather | solution.py:49
  256.7 1.6 stack.2
  258.3 6.7 all-to-all-start
  265.1 48.9 %all-gather = f32[64,12,96]{2,1,0:T(8,128)S(1)} all-gather(f32[1,12,96]{2,1,0:T(8,128)S(1)} %bitcast.55), channel_id=1, replica_groups=mesh['dp'=64,'mp'=8] {'dp'}, dimensions={0}, use_global_device_ids=true | all-gather | bytes 299520 | tf_op jit(solution)/shard_map/all_gather | solution.py:50
  314.0 0.8 reshape.28
  314.8 1.9 copy.24
  316.8 3.2 reshape.35
  320.0 4.1 all-to-all-done
  324.1 1.6 fusion.3
  325.7 1.8 multiply_reduce_fusion.1
  327.6 2.4 fusion.2
  330.0 9.9 %all-gather.22.cloned.1.call-done = bf16[768,768]{0,1:T(8,128)(2,1)} async-done(((bf16[768,96]{0,1:T(8,128)(2,1)}), bf16[768,768]{0,1:T(8,128)(2,1)}) %all-gather.22.cloned.1.call-update) | async-done | bytes 1179664 | tf_op jit(solution)/shard_map/all_gather | solution.py:58
  339.8 2.4 multiply_reduce_fusion
  342.3 16.4 %all-reduce.2 = (f32[]{:T(128)}, f32[]{:T(128)}) all-reduce(f32[]{:T(128)} %get-tuple-element.38, f32[]{:T(128)} %get-tuple-element.40), channel_id=1, replica_groups=mesh['dp'=64,'mp'=8] {'mp'}, use_global_device_ids=true, to_apply=%region_5.0 | all-reduce | flops 2 | bytes 16 | tf_op jit(solution)/shard_map/psum | solution.py:106
  359.3 0.7 multiply_convert_fusion.1
  360.8 0.7 multiply_convert_fusion
  361.8 2.8 fusion.35
  364.6 0.3 fusion.26
  365.0 19.2 %all-gather.14.cloned.1.call-done = f32[768,768]{0,1:T(8,128)} async-done(((f32[768,96]{0,1:T(8,128)}), f32[768,768]{0,1:T(8,128)}) %all-gather.14.cloned.1.call-update) | async-done | bytes 2359312 | tf_op jit(solution)/shard_map/all_gather | solution.py:57
  384.2 3.7 fusion.34
  387.9 0.3 convolution_divide_fusion
  388.2 0.3 convolution_bitcast_fusion.1
  388.5 1.0 copy.30
  389.5 37.8 %all-gather.16.cloned.1.call-done = bf16[768,768]{1,0:T(8,128)(2,1)} async-done(((bf16[96,768]{1,0:T(8,128)(2,1)}), bf16[768,768]{1,0:T(8,128)(2,1)}) %all-gather.16.cloned.1.call-update) | async-done | bytes 1179664 | tf_op jit(solution)/shard_map/all_gather | solution.py:29
  427.3 2.4 convolution_convert_fusion.3
  429.9 40.4 %all-gather.24.cloned.1.call-done = bf16[768,768]{1,0:T(8,128)(2,1)} async-done(((bf16[96,768]{1,0:T(8,128)(2,1)}), bf16[768,768]{1,0:T(8,128)(2,1)}) %all-gather.24.cloned.1.call-update) | async-done | bytes 1179664 | tf_op jit(solution)/shard_map/all_gather | solution.py:29
  470.3 2.4 convolution_convert_fusion.1
  472.8 38.7 %reduce-scatter.5.cloned.1.call-done = f32[96,12]{1,0:T(8,128)} async-done(((f32[768,12]{1,0:T(8,128)}), f32[96,12]{1,0:T(8,128)}) %reduce-scatter.5.cloned.1.call-update) | async-done | bytes 4624
  511.5 1.9 convolution_bitcast_fusion
  513.5 41.1 %all-gather.18.cloned.1.call-done = bf16[768,768]{1,0:T(8,128)(2,1)} async-done(((bf16[96,768]{1,0:T(8,128)(2,1)}), bf16[768,768]{1,0:T(8,128)(2,1)}) %all-gather.18.cloned.1.call-update) | async-done | bytes 1179664 | tf_op jit(solution)/shard_map/all_gather | solution.py:29
  554.6 2.5 fusion.9
  557.3 39.7 %all-gather.26.cloned.1.call-done = bf16[768,768]{1,0:T(8,128)(2,1)} async-done(((bf16[96,768]{1,0:T(8,128)(2,1)}), bf16[768,768]{1,0:T(8,128)(2,1)}) %all-gather.26.cloned.1.call-update) | async-done | bytes 1179664 | tf_op jit(solution)/shard_map/all_gather | solution.py:29
  597.0 2.5 fusion.11
  599.7 187.4 %all-reduce.8.cloned.1.call-done = f32[768,96]{0,1:T(8,128)} async-done(((f32[768,96]{0,1:T(8,128)}), f32[768,96]{0,1:T(8,128)}) %all-reduce.8.cloned.1.call-update) | async-done | bytes 294928
  787.0 1.0 convert_bitcast_fusion
  788.1 41.5 %all-gather.2 = bf16[64,12,96]{2,1,0:T(8,128)(2,1)S(1)} all-gather(bf16[1,12,96]{2,1,0:T(8,128)(2,1)S(1)} %copy.27), channel_id=1, replica_groups=mesh['dp'=64,'mp'=8] {'dp'}, dimensions={0}, use_global_device_ids=true | all-gather | bytes 149760 | tf_op jit(solution)/shard_map/all_gather | solution.py:84
  829.6 0.8 copy.28
  830.4 0.7 copy.29
  831.1 3.1 fusion.6
  834.2 38.1 %all-gather.28.cloned.1.call-done = bf16[768,768]{1,0:T(8,128)(2,1)} async-done(((bf16[96,768]{1,0:T(8,128)(2,1)}), bf16[768,768]{1,0:T(8,128)(2,1)}) %all-gather.28.cloned.1.call-update) | async-done | bytes 1179664 | tf_op jit(solution)/shard_map/all_gather | solution.py:29
  872.3 3.2 fusion.4
  (75 shorter events, 1.6 us)
Async XLA Ops:
  7.2 2.2 copy-start.13
  7.2 2.9 copy-start
  7.2 200.5 %copy-start.21 = (f32[12,96]{1,0:T(8,128)S(1)}, f32[12,96]{1,0:T(8,128)}, u32[]{:S(2)}) copy-start(f32[12,96]{1,0:T(8,128)} %param.10) | copy-start | bytes 13828
  7.2 200.4 %all-reduce.6.cloned.1.call-start = ((), (), s32[]{:S(2)}) async-start(), calls=%async_computation.12 | async-start | bytes 786432
  9.3 307.5 %all-gather.30.cloned.1.call-start = ((), (), s32[]{:S(2)}) async-start(), calls=%async_computation.10 | async-start | bytes 1597440 | tf_op jit(solution)/shard_map/all_gather | solution.py:51
  10.0 329.8 %all-gather.22.cloned.1.call-start = ((), (), s32[]{:S(2)}) async-start(), calls=%async_computation.6 | async-start | bytes 1327104 | tf_op jit(solution)/shard_map/all_gather | solution.py:58
  208.4 56.7 %copy-start.17 = (f32[12,96]{1,0:T(8,128)}, f32[12,96]{1,0:T(8,128)S(1)}, u32[]{:S(2)}) copy-start(f32[12,96]{1,0:T(8,128)S(1)} %get-tuple-element.37) | copy-start | bytes 13828
  258.3 65.8 %all-to-all-start = ((f32[8,768,96]{1,2,0:T(8,128)}), f32[8,768,96]{1,2,0:T(8,128)S(1)}, u32[]{:S(2)}, u32[]{:S(2)}) async-start(f32[8,768,96]{1,2,0:T(8,128)} %stack.2), calls=%async_computation | async-start | bytes 4718592 | tf_op jit(solution)/shard_map/all_to_all | solution.py:55
  265.0 119.1 %all-gather.14.cloned.1.call-start = ((), (), s32[]{:S(2)}) async-start(), calls=%async_computation.2 | async-start | bytes 2654208 | tf_op jit(solution)/shard_map/all_gather | solution.py:57
  316.7 110.7 %all-gather.16.cloned.1.call-start = ((), (), s32[]{:S(2)}) async-start(), calls=%async_computation.3 | async-start | bytes 1327104 | tf_op jit(solution)/shard_map/all_gather | solution.py:29
  316.7 7.3 copy-start.15
  324.1 1.6 copy-start.3
  325.7 4.2 copy-start.10
  325.7 1.8 copy-start.16
  329.9 30.1 %copy-start.11 = (f32[96,768]{1,0:T(8,128)}, f32[96,768]{1,0:T(8,128)S(1)}, u32[]{:S(2)}) copy-start(f32[96,768]{1,0:T(8,128)S(1)} %fusion.2) | copy-start | bytes 884740
  339.8 19.5 %copy-start.12 = (f32[96,768]{1,0:T(8,128)S(1)}, f32[96,768]{1,0:T(8,128)}, u32[]{:S(2)}) copy-start(f32[96,768]{1,0:T(8,128)} %get-tuple-element.39) | copy-start | bytes 884740
  360.1 110.2 %all-gather.24.cloned.1.call-start = ((), (), s32[]{:S(2)}) async-start(), calls=%async_computation.7 | async-start | bytes 1327104 | tf_op jit(solution)/shard_map/all_gather | solution.py:29
  361.5 3.1 copy-start.19
  361.5 22.6 %copy-start.14 = (f32[768,12]{0,1:T(8,128)S(1)}, f32[768,12]{0,1:T(8,128)}, u32[]{:S(2)}) copy-start(f32[768,12]{0,1:T(8,128)} %param.12) | copy-start | bytes 110596
  361.5 150.0 %reduce-scatter.5.cloned.1.call-start = ((), (), s32[]{:S(2)}) async-start(), calls=%async_computation.11 | async-start | bytes 442368
  364.9 22.9 %copy-start.18 = (f32[12,96]{1,0:T(8,128)}, f32[12,96]{1,0:T(8,128)S(1)}, u32[]{:S(2)}) copy-start(f32[12,96]{1,0:T(8,128)S(1)} %fusion.26) | copy-start | bytes 13828
  387.9 39.5 %copy-start.4 = (bf16[96,768]{1,0:T(8,128)(2,1)S(1)}, bf16[96,768]{1,0:T(8,128)(2,1)}, u32[]{:S(2)}) copy-start(bf16[96,768]{1,0:T(8,128)(2,1)} %multiply_convert_fusion.1) | copy-start | bytes 442372
  388.5 81.8 %copy-start.5 = (bf16[96,768]{1,0:T(8,128)(2,1)S(1)}, bf16[96,768]{1,0:T(8,128)(2,1)}, u32[]{:S(2)}) copy-start(bf16[96,768]{1,0:T(8,128)(2,1)} %multiply_convert_fusion) | copy-start | bytes 442372
  389.5 165.1 %all-gather.18.cloned.1.call-start = ((), (), s32[]{:S(2)}) async-start(), calls=%async_computation.4 | async-start | bytes 1327104 | tf_op jit(solution)/shard_map/all_gather | solution.py:29
  429.8 124.8 %copy-start.1 = (bf16[768,768]{1,0:T(8,128)(2,1)S(1)}, bf16[768,768]{1,0:T(8,128)(2,1)}, u32[]{:S(2)}) copy-start(bf16[768,768]{1,0:T(8,128)(2,1)} %all-gather.16.cloned.1.call-done) | copy-start | bytes 3538948
  429.8 124.8 %copy-start.8 = (bf16[96,768]{1,0:T(8,128)(2,1)S(1)}, bf16[96,768]{1,0:T(8,128)(2,1)}, u32[]{:S(2)}) copy-start(bf16[96,768]{1,0:T(8,128)(2,1)} %convolution_convert_fusion.3) | copy-start | bytes 442372
  429.8 167.1 %all-gather.26.cloned.1.call-start = ((), (), s32[]{:S(2)}) async-start(), calls=%async_computation.8 | async-start | bytes 1327104 | tf_op jit(solution)/shard_map/all_gather | solution.py:29
  472.8 314.2 %all-reduce.8.cloned.1.call-start = ((), (), s32[]{:S(2)}) async-start(), calls=%async_computation.13 | async-start | bytes 589824
  513.4 83.5 %copy-start.2 = (bf16[768,768]{1,0:T(8,128)(2,1)S(1)}, bf16[768,768]{1,0:T(8,128)(2,1)}, u32[]{:S(2)}) copy-start(bf16[768,768]{1,0:T(8,128)(2,1)} %all-gather.24.cloned.1.call-done) | copy-start | bytes 3538948
  513.5 83.5 %copy-start.7 = (bf16[96,768]{1,0:T(8,128)(2,1)S(1)}, bf16[96,768]{1,0:T(8,128)(2,1)}, u32[]{:S(2)}) copy-start(bf16[96,768]{1,0:T(8,128)(2,1)} %convolution_convert_fusion.1) | copy-start | bytes 442372
  513.5 317.6 %all-gather.20.cloned.1.call-start = ((), (), s32[]{:S(2)}) async-start(), calls=%async_computation.5 | async-start | bytes 1327104 | tf_op jit(solution)/shard_map/all_gather | solution.py:29
  557.2 42.3 %copy-start.20 = (f32[12,96]{1,0:T(8,128)S(1)}, f32[12,96]{1,0:T(8,128)}, u32[]{:S(2)}) copy-start(f32[12,96]{1,0:T(8,128)} %param.9) | copy-start | bytes 13828
  557.2 315.1 %all-gather.28.cloned.1.call-start = ((), (), s32[]{:S(2)}) async-start(), calls=%async_computation.9 | async-start | bytes 1327104 | tf_op jit(solution)/shard_map/all_gather | solution.py:29
  599.5 231.6 %copy-start.6 = (bf16[96,768]{1,0:T(8,128)(2,1)S(1)}, bf16[96,768]{1,0:T(8,128)(2,1)}, u32[]{:S(2)}) copy-start(bf16[96,768]{1,0:T(8,128)(2,1)} %fusion.9) | copy-start | bytes 442372
  831.1 41.2 %copy-start.9 = (bf16[96,768]{1,0:T(8,128)(2,1)S(1)}, bf16[96,768]{1,0:T(8,128)(2,1)}, u32[]{:S(2)}) copy-start(bf16[96,768]{1,0:T(8,128)(2,1)} %fusion.11) | copy-start | bytes 442372
Sparse Core Ops, SparseCore 0:
  11.5 196.1 all-reduce.5
  212.1 80.6 all-gather.29
  295.6 44.1 all-gather.21
  342.5 41.5 all-gather.13
  386.9 40.4 all-gather.15
  430.1 40.2 all-gather.23
  473.3 38.1 reduce-scatter.4
  514.2 40.4 all-gather.17
  556.7 40.2 all-gather.25
  600.9 186.1 all-reduce.7
  789.9 39.8 all-gather.19
  832.0 40.2 all-gather.27
